TPU v7x, 512 devices: a whole 4x8x8 slice. The times are simulated.
512 devices in a mesh: rep: 8 (over y_lo, core), seq: 2 (over y_hi), tp: 32 (over x, z).
Axes of the slice: x: 4, y: 8 (y_hi: 2, y_lo: 4; y = y_hi * 4 + y_lo), z: 8, core: 2. Of those that a mesh axis runs over, the one named last changes fastest.
Arguments:
- hidden: bfloat16 [3072, 8192], P('rep', ('seq', 'tp')), may hold values from -100 to 100
- gain: float32 [8192], replicated, may hold values from 0.1 to 1.9
- w_query: bfloat16 [8192, 8192], P('seq', 'tp'), may hold values from -1 to 1
- w_keyval: bfloat16 [2, 4096, 2048], P(None, 'tp'), may hold values from -1 to 1
- lengths: int32 [8, 2], replicated, may hold values from 128 to 192, as said below
- routes: int32 [8, 2], replicated, may hold values from 0 to 7, as said below
Outputs:
- attended: bfloat16 [3072, 8192], P(('rep', 'seq'), 'tp')
Inputs may be any that keep to these rules, and one draw needn't show every extreme that they name: `routes`: for each j, the responses j of the 8 rollout groups go to 8 different replicas, so each replica receives exactly 2 responses. `lengths`: the responses that one rollout group sends to one replica hold at most 192 tokens together, and in every draw some group sends exactly 192 tokens to one replica.
All inputs are finite; a program needn't handle non-finite values.
Results may differ from a plain program's by a relative error of at most 0.0076.
Values may be sent and summed in bfloat16 or wider, within the bound.
No kernel may reach another device: no remote copies, remote signals or barrier semaphores. Data moves between devices by JAX's collectives and lax.ppermute only.
A program may use at most 64 MiB of HBM per device.

v0:
```python
import math
import jax
import jax.numpy as jnp
from jax import lax
from jax.sharding import PartitionSpec as P

D = 8192
QH = 64
KVH = 8
HD = 128
RESP = 2
LMAX = 192
BUFFER = 384
ROPE_BASE = 500000.0
NORM_EPS = 1e-05
MASK_FILL = -1e30


def response_tables(lengths, routes):
    flat_len = lengths.reshape(-1)
    flat_route = routes.reshape(-1)
    response_ids = jnp.arange(flat_len.shape[0], dtype=jnp.int32)
    group_of = response_ids // RESP
    same_route = flat_route[:, None] == flat_route[None, :]
    same_group = group_of[:, None] == group_of[None, :]
    earlier = response_ids[None, :] < response_ids[:, None]
    dest_off = jnp.sum(jnp.where(same_route & earlier, flat_len[None, :], 0), axis=1)
    pair_off = jnp.sum(jnp.where(same_route & same_group & earlier, flat_len[None, :], 0), axis=1)
    src_start = jnp.sum(jnp.where(same_group & earlier, flat_len[None, :], 0), axis=1)
    return (flat_len, flat_route, group_of, dest_off, pair_off, src_start)


def locate(positions, replica, tables):
    flat_len, flat_route, group_of, dest_off, pair_off, src_start = tables
    response_ids = jnp.arange(flat_len.shape[0], dtype=jnp.int32)
    position_col = positions[:, None]
    inside = (
        (flat_route[None, :] == replica)
        & (dest_off[None, :] <= position_col)
        & (position_col < dest_off[None, :] + flat_len[None, :])
    )
    inside_int = inside.astype(jnp.int32)
    segment = jnp.sum(inside_int * (response_ids[None, :] + 1), axis=1) - 1
    seg_start = jnp.sum(inside_int * dest_off[None, :], axis=1)
    source_group = jnp.sum(inside_int * group_of[None, :], axis=1)
    pair_first = jnp.sum(inside_int * (dest_off - pair_off)[None, :], axis=1)
    source = jnp.sum(inside_int * src_start[None, :], axis=1)
    within = jnp.where(segment >= 0, positions - seg_start, 0)
    return (segment, within, source_group, pair_first, source)


def rotary(values_in, within):
    head_dim = values_in.shape[-1]
    half_dim = head_dim // 2
    freq_index = jnp.arange(half_dim, dtype=jnp.float32)
    inverse = jnp.power(ROPE_BASE, -2.0 * freq_index / head_dim)
    angles = within.astype(jnp.float32)[:, None] * inverse[None, :]
    cosine = jnp.cos(angles)[:, None, :]
    sine_part = jnp.sin(angles)[:, None, :]
    lower_half = values_in[..., :half_dim]
    upper_half = values_in[..., half_dim:]
    return jnp.concatenate(
        [
            lower_half * cosine - upper_half * sine_part,
            upper_half * cosine + lower_half * sine_part,
        ],
        axis=-1,
    )


def fill_rows(table, indices, present):
    taken = jnp.take(table, indices.reshape(-1), axis=0)
    return jnp.where(present.reshape(-1)[:, None], taken, jnp.zeros((), table.dtype))


def local(hidden, gain, w_query, w_keyval, lengths, routes):
    rep_count = lax.axis_size("rep")
    seq_count = lax.axis_size("seq")
    replica = lax.axis_index("rep")
    seq_index = lax.axis_index("seq")
    column = lax.axis_index("tp")
    feature_cols = hidden.shape[1]
    local_rows = BUFFER // seq_count
    capacity = (RESP + rep_count - 1) // rep_count * LMAX
    head_count = w_query.shape[1] // HD
    tables = response_tables(lengths, routes)
    flat_len, flat_route, group_of, dest_off, pair_off, src_start = tables
    my_len = lax.dynamic_slice_in_dim(flat_len, replica * RESP, RESP)
    my_route = lax.dynamic_slice_in_dim(flat_route, replica * RESP, RESP)
    my_pair = lax.dynamic_slice_in_dim(pair_off, replica * RESP, RESP)
    my_start = lax.dynamic_slice_in_dim(src_start, replica * RESP, RESP)
    slot_ids = jnp.arange(capacity, dtype=jnp.int32)
    targets = jnp.arange(rep_count, dtype=jnp.int32)
    block_off = jnp.broadcast_to(slot_ids[None, :], (rep_count, capacity))
    offsets = block_off[:, :, None]
    inside = (
        (my_route[None, None, :] == targets[:, None, None])
        & (my_pair[None, None, :] <= offsets)
        & (offsets < (my_pair + my_len)[None, None, :])
    )
    inside_int = inside.astype(jnp.int32)
    src_rows = jnp.sum(
        inside_int * (my_start[None, None, :] + offsets - my_pair[None, None, :]), axis=2
    )
    src_rows, present = (src_rows, jnp.any(inside, axis=2))
    outgoing = fill_rows(hidden, src_rows, present)
    incoming = lax.all_to_all(outgoing, "rep", split_axis=0, concat_axis=0, tiled=True)
    all_pos = jnp.arange(BUFFER, dtype=jnp.int32)
    segment, within, source_group, pair_first, source = locate(all_pos, replica, tables)
    gathered_idx = jnp.where(segment >= 0, source_group * capacity + all_pos - pair_first, 0)
    assembled = fill_rows(incoming, gathered_idx, segment >= 0)
    local_x = lax.all_to_all(
        assembled.reshape(BUFFER, 1, feature_cols), "seq", split_axis=0, concat_axis=1, tiled=True
    )
    query_pos = seq_index * local_rows + jnp.arange(local_rows, dtype=jnp.int32)
    query_info = locate(query_pos, replica, tables)
    query_seg = query_info[0]
    query_within = query_info[1]
    query_valid = query_seg >= 0
    gain_halves = gain.reshape(seq_count, D // seq_count)
    gain_local = lax.dynamic_slice_in_dim(gain_halves, column * feature_cols, feature_cols, 1)
    kv_head = column * head_count // (QH // KVH)
    query_weights = lax.all_gather(
        w_query.reshape(1, w_query.shape[0], w_query.shape[1]), "seq", axis=0, tiled=True
    )
    feature_piece = lax.all_gather(local_x, "tp", axis=2, tiled=True)
    scaled_piece = (feature_piece.astype(jnp.float32) * gain_halves[None]).astype(jnp.bfloat16)
    query_acc = jnp.einsum(
        "rsn,snf->rf", scaled_piece, query_weights, preferred_element_type=jnp.float32
    )
    squares = jnp.sum(jnp.square(feature_piece.astype(jnp.float32)), axis=(1, 2))
    inverse_rms = lax.rsqrt(squares / D + NORM_EPS)
    queries = rotary(
        inverse_rms[:, None, None] * query_acc.reshape(local_rows, head_count, HD), query_within
    ).astype(jnp.bfloat16)
    scaled_local = (local_x.astype(jnp.float32) * gain_local[None]).astype(jnp.bfloat16)
    kv_partial = jnp.einsum(
        "rsw,swc->rc", scaled_local, w_keyval, preferred_element_type=jnp.float32
    )
    kv_total = lax.psum(kv_partial, "tp")
    head_block = lax.dynamic_slice_in_dim(kv_total, kv_head * 2 * HD, 2 * HD, 1)
    keys = rotary(inverse_rms[:, None, None] * head_block[:, None, :HD], query_within)[:, 0].astype(
        jnp.bfloat16
    )
    values = (inverse_rms[:, None] * head_block[:, HD:]).astype(jnp.bfloat16)
    score_scale = 1.0 / math.sqrt(HD)
    running = jnp.full((local_rows, head_count), MASK_FILL, jnp.float32)
    key_part = lax.all_gather(keys, "seq", axis=0, tiled=True)
    value_part = lax.all_gather(values, "seq", axis=0, tiled=True)
    key_count = key_part.shape[0]
    key_pos = jnp.arange(key_count, dtype=jnp.int32)
    key_seg = locate(key_pos, replica, tables)[0]
    allowed = (key_seg[None, :] == query_seg[:, None]) & query_valid[:, None] & (
        key_pos[None, :] <= query_pos[:, None]
    ) | (key_pos[None, :] == query_pos[:, None])
    scores = (
        jnp.einsum("rhd,kd->rhk", queries, key_part, preferred_element_type=jnp.float32)
        * score_scale
    )
    scores = jnp.where(allowed[:, None, :], scores, MASK_FILL)
    new_max = jnp.maximum(running, jnp.max(scores, axis=2))
    prob_terms = jnp.where(allowed[:, None, :], jnp.exp(scores - new_max[:, :, None]), 0.0)
    totals = jnp.sum(prob_terms, axis=2)
    accum = jnp.einsum(
        "rhk,kd->rhd",
        prob_terms.astype(jnp.bfloat16),
        value_part,
        preferred_element_type=jnp.float32,
    )
    attended = (
        (accum / totals[:, :, None]).reshape(local_rows, head_count * HD).astype(jnp.bfloat16)
    )
    return jnp.where(query_valid[:, None], attended, jnp.zeros((), jnp.bfloat16))


def solution(mesh):
    in_specs = (P("rep", ("seq", "tp")), P(), P("seq", "tp"), P(None, "tp", None), P(), P())
    out_specs = P(("rep", "seq"), "tp")
    return jax.shard_map(local, mesh=mesh, in_specs=in_specs, out_specs=out_specs, check_vma=False)
```

profile of v0, /device:TPU:16, one launch (start us, length us, event | category | flops | bytes accessed | tf_op | source)
XLA Modules:
  0.0 440.9 jit_solution(4229495986316716021)
XLA Ops:
  6.5 0.8 copy.25
  7.4 0.1 broadcast_in_dim.98
  7.5 0.8 copy.24
  8.2 0.1 broadcast_in_dim_reshape.2
  8.3 0.1 dynamic_slice.18
  8.4 0.2 select_reduce_fusion.7
  8.6 0.1 dynamic-slice_add_fusion
  8.7 0.1 dynamic_slice.21
  8.8 0.1 iota_compare_fusion.7
  8.8 0.1 select_reduce_fusion.4
  8.9 0.1 reshape.451
  9.0 0.1 fusion.43
  9.1 3.5 gather_fusion
  12.7 1.3 select_select_fusion
  14.0 9.1 %all-to-all-start = ((bf16[8,192,128]{2,1,0:T(8,128)(2,1)}), bf16[8,192,128]{2,1,0:T(8,128)(2,1)S(1)}, u32[]{:S(2)}, u32[]{:S(2)}) async-start(bf16[8,192,128]{2,1,0:T(8,128)(2,1)} %select_select_fusion), calls=%async_computation | async-start | bytes 786432 | tf_op jit(solution)/shard_map/all_to_all | solution.py:107
  23.1 0.1 select_reduce_fusion.1
  23.3 9.1 %all-to-all-done = bf16[8,192,128]{2,1,0:T(8,128)(2,1)S(1)} async-done(((bf16[8,192,128]{2,1,0:T(8,128)(2,1)}), bf16[8,192,128]{2,1,0:T(8,128)(2,1)S(1)}, u32[]{:S(2)}, u32[]{:S(2)}) %all-to-all-start) | async-done | bytes 393248 | tf_op jit(solution)/shard_map/all_to_all | solution.py:107
  32.4 1.4 gather_fusion.1
  33.8 0.2 fusion.37
  34.0 0.5 broadcast.494
  34.5 0.7 reduce.4
  35.2 10.6 %all_to_all.27 = bf16[2,2,12288]{2,1,0:T(2,128)(2,1)S(1)} all-to-all(bf16[2,2,12288]{2,1,0:T(2,128)(2,1)S(1)} %reshape.481), channel_id=1, replica_groups=mesh['rep'=8,'seq'=2,'tp'=32] {'seq'}, dimensions={0} | all-to-all | bytes 196608 | tf_op jit(solution)/shard_map/all_to_all | solution.py:112
  45.8 0.1 reshape.482
  45.9 0.7 copy.29
  46.5 0.0 all-gather.6.cloned.1.call-update
  46.6 0.0 all-gather.8.cloned.1.call-start
  46.6 0.7 all-gather.8.cloned.1.call-update
  47.3 0.0 all-reduce.2.cloned.1.call-start
  47.5 0.1 select_reduce_fusion.3
  47.6 0.2 fusion.18
  47.8 2.5 convolution_bitcast_fusion
  50.3 0.4 multiply_cosine_fusion.1
  50.7 82.6 %all-gather.6.cloned.1.call-done = bf16[192,2,1,4096]{3,0,1,2:T(8,128)(2,1)} async-done(((bf16[192,2,1,128]{3,0,1,2:T(8,128)(2,1)}), bf16[192,2,1,4096]{3,0,1,2:T(8,128)(2,1)}) %all-gather.6.cloned.1.call-update) | async-done | bytes 3145744 | tf_op jit(solution)/shard_map/all_gather | solution.py:126
  133.3 2.6 fusion
  135.9 111.5 %all-gather.8.cloned.1.call-done = bf16[8192,256]{1,0:T(8,128)(2,1)} async-done(((bf16[4096,256]{1,0:T(8,128)(2,1)}), bf16[8192,256]{1,0:T(8,128)(2,1)}) %all-gather.8.cloned.1.call-update) | async-done | bytes 4194320 | tf_op jit(solution)/shard_map/all_gather | solution.py:123
  247.4 4.1 fusion.7
  251.6 0.1 bitcast_multiply_fusion
  251.7 161.3 %all-reduce.2.cloned.1.call-done = f32[192,2048]{1,0:T(8,128)} async-done(((f32[192,2048]{1,0:T(8,128)}), f32[192,2048]{1,0:T(8,128)}) %all-reduce.2.cloned.1.call-update) | async-done | bytes 1572880 | tf_op jit(solution)/shard_map/psum | solution.py:140
  412.9 1.0 fusion.30
  413.9 0.5 fusion.26
  414.4 0.1 pad_maximum_fusion
  414.5 9.2 %all-gather.2 = bf16[384,1,128]{2,0,1:T(8,128)(2,1)S(1)} all-gather(bf16[192,1,128]{2,0,1:T(8,128)(2,1)S(1)} %pad_maximum_fusion), channel_id=4, replica_groups=mesh['rep'=8,'seq'=2,'tp'=32] {'seq'}, dimensions={0}, use_global_device_ids=true | all-gather | bytes 147456 | tf_op jit(solution)/shard_map/all_gather | solution.py:148
  423.7 0.1 subtract_convert_fusion
  423.9 0.4 fusion.50
  424.3 8.7 %all_gather.15 = bf16[384,128]{1,0:T(8,128)(2,1)S(1)} all-gather(bf16[192,128]{1,0:T(8,128)(2,1)S(1)} %get-tuple-element.19), channel_id=1, replica_groups=mesh['rep'=8,'seq'=2,'tp'=32] {'seq'}, dimensions={0}, use_global_device_ids=true | all-gather | bytes 147456 | tf_op jit(solution)/shard_map/all_gather | solution.py:149
  433.0 0.3 fusion.12
  433.3 0.3 fusion.11
  433.7 0.7 bitcast_select_fusion
  (25 shorter events, 0.2 us)
Async XLA Ops:
  6.5 41.2 %copy-start = (bf16[2,128,2048]{2,1,0:T(8,128)(2,1)S(1)}, bf16[2,128,2048]{2,1,0:T(8,128)(2,1)}, u32[]{:S(2)}) copy-start(bf16[2,128,2048]{2,1,0:T(8,128)(2,1)} %param.9) | copy-start | bytes 3145732
  12.7 34.7 %copy-start.1 = (f32[8192]{0:T(1024)S(1)}, f32[8192]{0:T(1024)}, u32[]{:S(2)}) copy-start(f32[8192]{0:T(1024)} %param.7) | copy-start | bytes 98308
  14.0 18.4 %all-to-all-start = ((bf16[8,192,128]{2,1,0:T(8,128)(2,1)}), bf16[8,192,128]{2,1,0:T(8,128)(2,1)S(1)}, u32[]{:S(2)}, u32[]{:S(2)}) async-start(bf16[8,192,128]{2,1,0:T(8,128)(2,1)} %select_select_fusion), calls=%async_computation | async-start | bytes 786432 | tf_op jit(solution)/shard_map/all_to_all | solution.py:107
  23.1 110.2 %all-gather.6.cloned.1.call-start = ((), (), s32[]{:S(2)}) async-start(), calls=%async_computation.3 | async-start | bytes 3244032 | tf_op jit(solution)/shard_map/all_gather | solution.py:126
  46.6 200.9 %all-gather.8.cloned.1.call-start = ((), (), s32[]{:S(2)}) async-start(), calls=%async_computation.4 | async-start | bytes 6291456 | tf_op jit(solution)/shard_map/all_gather | solution.py:123
  47.3 365.6 %all-reduce.2.cloned.1.call-start = ((), (), s32[]{:S(2)}) async-start(), calls=%async_computation.2 | async-start | bytes 3145728 | tf_op jit(solution)/shard_map/psum | solution.py:140
Sparse Core Ops, SparseCore 0:
  46.7 86.6 all-gather.5
  135.4 111.9 all-gather.7
  250.8 162.0 all-reduce.1
where the time goes:
time: 441 us
  waiting for transfers between devices  365 us (83%)
  blocking collectives  28.5 us (6%)
  between operations  13.4 us (3%)
  starting transfers between devices  9.17 us (2%)
  other arithmetic  9.02 us (2%)
  local copies, waits for them, and re-layouts  8.3 us (2%)
  matrix products  7.34 us (2%)
    psum x1, waiting for transfers between devices, local(): kv_total = lax.psum(kv_partial, 'tp')  161 us
    all_gather x1, waiting for transfers between devices, local(): lax.all_gather(w_query.reshape(1, w_query.shape[0], w_query.shape[1]), 's...  111 us
    all_gather x1, waiting for transfers between devices, local(): feature_piece = lax.all_gather(local_x, 'tp', axis=2, tiled=True)  82.6 us
    all_to_all x1, blocking collectives, local(): lax.all_to_all(assembled.reshape(BUFFER, 1, feature_cols), 'seq', split_a...  10.6 us
    all_gather x1, blocking collectives, local(): key_part = lax.all_gather(keys, 'seq', axis=0, tiled=True)  9.25 us
    all_to_all x1, waiting for transfers between devices, local(): lax.all_to_all(outgoing, 'rep', split_axis=0, concat_axis=0, tiled=True)  9.09 us
    all_to_all x1, starting transfers between devices, local(): lax.all_to_all(outgoing, 'rep', split_axis=0, concat_axis=0, tiled=True)  9.08 us
  transfers between devices with their start and end apart: 4, of which 4 were waited for; matrix products, arithmetic and copies ran while one was open for 2% of the time, Pallas kernels for 0%

commit v1 on v0

--- a/solution.py
+++ b/solution.py
@@ -137,7 +137,7 @@
     kv_partial = jnp.einsum(
         "rsw,swc->rc", scaled_local, w_keyval, preferred_element_type=jnp.float32
     )
-    kv_total = lax.psum(kv_partial, "tp")
+    kv_total = jnp.sum(lax.all_gather(kv_partial, "tp"), axis=0)
     head_block = lax.dynamic_slice_in_dim(kv_total, kv_head * 2 * HD, 2 * HD, 1)
     keys = rotary(inverse_rms[:, None, None] * head_block[:, None, :HD], query_within)[:, 0].astype(
         jnp.bfloat16

time: 441 us -> 633 us (1.44)
  waiting for transfers between devices: 365 us -> 540 us
  other arithmetic: 9.02 us -> 25.2 us
    all_gather x0 -> x1, waiting for transfers between devices: none -> 337 us  [local(): kv_total = jnp.sum(lax.all_gather(kv_partial, 'tp'), axis=0)]
    psum x1 -> x0, waiting for transfers between devices: 161 us -> none  [local(): kv_total = lax.psum(kv_partial, 'tp')]
    reduce_sum x0 -> x1, other arithmetic: none -> 17.1 us  [local(): kv_total = jnp.sum(lax.all_gather(kv_partial, 'tp'), axis=0)]
where the time goes in v1:
time: 633 us; the launch traced here: 632 us
  waiting for transfers between devices  540 us (85%)
  blocking collectives  28.5 us (5%)
  other arithmetic  25.2 us (4%)
  between operations  13.4 us (2%)
  starting transfers between devices  9.17 us (1%)
  local copies, waits for them, and re-layouts  8.31 us (1%)
  matrix products  7.37 us (1%)
    all_gather x1, waiting for transfers between devices, local(): kv_total = jnp.sum(lax.all_gather(kv_partial, 'tp'), axis=0)  337 us
    all_gather x1, waiting for transfers between devices, local(): lax.all_gather(w_query.reshape(1, w_query.shape[0], w_query.shape[1]), 's...  111 us
    all_gather x1, waiting for transfers between devices, local(): feature_piece = lax.all_gather(local_x, 'tp', axis=2, tiled=True)  82.6 us
    reduce_sum x1, other arithmetic, local(): kv_total = jnp.sum(lax.all_gather(kv_partial, 'tp'), axis=0)  17.1 us
  transfers between devices with their start and end apart: 4, of which 4 were waited for; matrix products, arithmetic and copies ran while one was open for 2% of the time, Pallas kernels for 0%

profile of v1, /device:TPU:16, one launch (start us, length us, event | category | flops | bytes accessed | tf_op | source)
XLA Modules:
  0.0 632.4 jit_solution(15979443122288139436)
XLA Ops:
  6.5 0.8 copy.25
  7.4 0.1 broadcast_in_dim.98
  7.5 0.8 copy.24
  8.2 0.1 broadcast_in_dim_reshape.2
  8.3 0.1 dynamic_slice.18
  8.4 0.2 select_reduce_fusion.7
  8.6 0.1 dynamic-slice_add_fusion
  8.7 0.1 dynamic_slice.21
  8.8 0.1 iota_compare_fusion.7
  8.8 0.1 select_reduce_fusion.4
  8.9 0.1 reshape.451
  9.0 0.1 fusion.43
  9.1 3.5 gather_fusion
  12.7 1.3 select_select_fusion
  14.0 9.1 %all-to-all-start = ((bf16[8,192,128]{2,1,0:T(8,128)(2,1)}), bf16[8,192,128]{2,1,0:T(8,128)(2,1)S(1)}, u32[]{:S(2)}, u32[]{:S(2)}) async-start(bf16[8,192,128]{2,1,0:T(8,128)(2,1)} %select_select_fusion), calls=%async_computation | async-start | bytes 786432 | tf_op jit(solution)/shard_map/all_to_all | solution.py:107
  23.1 0.1 select_reduce_fusion.1
  23.3 9.1 %all-to-all-done = bf16[8,192,128]{2,1,0:T(8,128)(2,1)S(1)} async-done(((bf16[8,192,128]{2,1,0:T(8,128)(2,1)}), bf16[8,192,128]{2,1,0:T(8,128)(2,1)S(1)}, u32[]{:S(2)}, u32[]{:S(2)}) %all-to-all-start) | async-done | bytes 393248 | tf_op jit(solution)/shard_map/all_to_all | solution.py:107
  32.4 1.4 gather_fusion.1
  33.8 0.2 fusion.37
  34.0 0.5 broadcast.494
  34.5 0.7 reduce.4
  35.2 10.6 %all_to_all.27 = bf16[2,2,12288]{2,1,0:T(2,128)(2,1)S(1)} all-to-all(bf16[2,2,12288]{2,1,0:T(2,128)(2,1)S(1)} %reshape.482), channel_id=1, replica_groups=mesh['rep'=8,'seq'=2,'tp'=32] {'seq'}, dimensions={0} | all-to-all | bytes 196608 | tf_op jit(solution)/shard_map/all_to_all | solution.py:112
  45.8 0.1 reshape.483
  45.9 0.7 copy.29
  46.6 0.0 all-gather.10.cloned.1.call-start
  46.6 0.7 all-gather.10.cloned.1.call-update
  47.3 0.0 all-gather.12.cloned.1.call-start
  47.4 2.5 convolution_bitcast_fusion
  50.0 0.1 select_reduce_fusion.3
  50.1 0.2 fusion.18
  50.3 0.4 multiply_cosine_fusion.1
  50.7 82.6 %all-gather.8.cloned.1.call-done = bf16[192,2,1,4096]{3,0,1,2:T(8,128)(2,1)} async-done(((bf16[192,2,1,128]{3,0,1,2:T(8,128)(2,1)}), bf16[192,2,1,4096]{3,0,1,2:T(8,128)(2,1)}) %all-gather.8.cloned.1.call-update) | async-done | bytes 3145744 | tf_op jit(solution)/shard_map/all_gather | solution.py:126
  133.3 2.6 fusion
  135.9 111.5 %all-gather.10.cloned.1.call-done = bf16[8192,256]{1,0:T(8,128)(2,1)} async-done(((bf16[4096,256]{1,0:T(8,128)(2,1)}), bf16[8192,256]{1,0:T(8,128)(2,1)}) %all-gather.10.cloned.1.call-update) | async-done | bytes 4194320 | tf_op jit(solution)/shard_map/all_gather | solution.py:123
  247.4 4.1 fusion.7
  251.6 0.1 bitcast_multiply_fusion
  251.7 0.1 subtract_convert_fusion
  251.8 336.6 %all-gather.12.cloned.1.call-done = f32[6144,2048]{1,0:T(8,128)} async-done(((f32[192,2048]{1,0:T(8,128)}), f32[6144,2048]{1,0:T(8,128)}) %all-gather.12.cloned.1.call-update) | async-done | bytes 50331664 | tf_op jit(solution)/shard_map/all_gather | solution.py:140
  588.4 17.1 %reduce_sum.125 = f32[192,2048]{1,0:T(8,128)S(1)} reduce(f32[32,192,2048]{2,1,0:T(8,128)} %bitcast.48, f32[]{:T(128)} %constant.113.clone.1), dimensions={0}, to_apply=%region_11.12 | reduce | flops 12189696 | bytes 51904516 | tf_op jit(solution)/shard_map/reduce_sum | solution.py:140
  605.5 0.1 fusion.30
  605.6 0.5 fusion.26
  606.0 0.1 pad_maximum_fusion
  606.1 9.2 %all-gather.3 = bf16[384,1,128]{2,0,1:T(8,128)(2,1)S(1)} all-gather(bf16[192,1,128]{2,0,1:T(8,128)(2,1)S(1)} %pad_maximum_fusion), channel_id=5, replica_groups=mesh['rep'=8,'seq'=2,'tp'=32] {'seq'}, dimensions={0}, use_global_device_ids=true | all-gather | bytes 147456 | tf_op jit(solution)/shard_map/all_gather | solution.py:148
  615.4 0.4 fusion.50
  615.8 8.7 %all_gather.23 = bf16[384,128]{1,0:T(8,128)(2,1)S(1)} all-gather(bf16[192,128]{1,0:T(8,128)(2,1)S(1)} %get-tuple-element.19), channel_id=1, replica_groups=mesh['rep'=8,'seq'=2,'tp'=32] {'seq'}, dimensions={0}, use_global_device_ids=true | all-gather | bytes 147456 | tf_op jit(solution)/shard_map/all_gather | solution.py:149
  624.5 0.3 fusion.12
  624.8 0.3 fusion.11
  625.1 0.7 bitcast_select_fusion
  (28 shorter events, 0.3 us)
Async XLA Ops:
  6.5 40.9 %copy-start = (bf16[2,128,2048]{2,1,0:T(8,128)(2,1)S(1)}, bf16[2,128,2048]{2,1,0:T(8,128)(2,1)}, u32[]{:S(2)}) copy-start(bf16[2,128,2048]{2,1,0:T(8,128)(2,1)} %param.9) | copy-start | bytes 3145732
  12.7 34.7 %copy-start.2 = (f32[8192]{0:T(1024)S(1)}, f32[8192]{0:T(1024)}, u32[]{:S(2)}) copy-start(f32[8192]{0:T(1024)} %param.7) | copy-start | bytes 98308
  14.0 18.4 %all-to-all-start = ((bf16[8,192,128]{2,1,0:T(8,128)(2,1)}), bf16[8,192,128]{2,1,0:T(8,128)(2,1)S(1)}, u32[]{:S(2)}, u32[]{:S(2)}) async-start(bf16[8,192,128]{2,1,0:T(8,128)(2,1)} %select_select_fusion), calls=%async_computation | async-start | bytes 786432 | tf_op jit(solution)/shard_map/all_to_all | solution.py:107
  23.1 110.2 %all-gather.8.cloned.1.call-start = ((), (), s32[]{:S(2)}) async-start(), calls=%async_computation.2 | async-start | bytes 3244032 | tf_op jit(solution)/shard_map/all_gather | solution.py:126
  46.6 200.9 %all-gather.10.cloned.1.call-start = ((), (), s32[]{:S(2)}) async-start(), calls=%async_computation.3 | async-start | bytes 6291456 | tf_op jit(solution)/shard_map/all_gather | solution.py:123
  47.3 541.1 %all-gather.12.cloned.1.call-start = ((), (), s32[]{:S(2)}) async-start(), calls=%async_computation.4 | async-start | bytes 51904512 | tf_op jit(solution)/shard_map/all_gather | solution.py:140
  588.4 37.5 %copy-start.1 = (bf16[2,128,2048]{2,1,0:T(8,128)(2,1)S(1)}, bf16[2,128,2048]{2,1,0:T(8,128)(2,1)}, u32[]{:S(2)}) copy-start(bf16[2,128,2048]{2,1,0:T(8,128)(2,1)} %param.9) | copy-start | bytes 3145732
Sparse Core Ops, SparseCore 0:
  46.7 86.6 all-gather.7
  135.4 111.9 all-gather.9
  250.6 337.7 all-gather.11
